TPU v7x, 256 devices: a whole 4x4x8 slice. The times are simulated.
256 devices in a mesh: blk: 128 (over z, x_hi, y, core), rows: 2 (over x_lo).
Axes of the slice: x: 4 (x_hi: 2, x_lo: 2; x = x_hi * 2 + x_lo), y: 4, z: 8, core: 2. Of those that a mesh axis runs over, the one named last changes fastest.
Arguments:
- tokens: bfloat16 [512, 8192], P(('blk', 'rows')), may hold values from -60 to 60
- norm_gain: float32 [8192], replicated, may hold values from 0.1 to 1.9
- gate_weight: bfloat16 [8192, 32768], P(None, 'blk'), may hold values from -0.09375 to 0.09375
- up_weight: bfloat16 [8192, 32768], P(None, 'blk'), may hold values from -0.09375 to 0.09375
- down_weight: bfloat16 [32768, 8192], P('blk'), may hold values from -0.046875 to 0.046875
- gate_mask: int32 [64, 256], P(None, 'blk'), may hold values from 0 to 1, as said below
- up_mask: int32 [64, 256], P(None, 'blk'), may hold values from 0 to 1, as said below
- down_mask: int32 [256, 64], P('blk'), may hold values 0 or 1
Outputs:
- ffn_out: bfloat16 [512, 8192], P(('blk', 'rows'))
Inputs may be any that keep to these rules, and one draw needn't show every extreme that they name: Each column of gate_mask (64 block flags) has between 16 and 48 ones, and some column has exactly 48. Each column of up_mask (64 block flags) has between 16 and 48 ones, and some column has exactly 48.
All inputs are finite; a program needn't handle non-finite values. No bound on the sum of `down_mask` on one device may be relied on, other than what follows from the above.
Results may differ from a plain program's by a relative error of at most 0.0065.
Values may be sent and summed in bfloat16 or wider, within the bound.
No kernel may reach another device: no remote copies, remote signals or barrier semaphores. Data moves between devices by JAX's collectives and lax.ppermute only.
A program may use at most 128 MiB of HBM per device.

v0:
```python
import jax
import jax.numpy as jnp
from jax import lax
from jax.sharding import PartitionSpec as P


def mask_blocks(weight, flags):
    height, width = weight.shape
    down_n = flags.shape[0]
    across_n = flags.shape[1]
    shaped = weight.reshape(down_n, height // down_n, across_n, width // across_n)
    return (shaped * flags.astype(weight.dtype)[:, None, :, None]).reshape(height, width)


def local(tokens, norm_gain, gate_weight, up_weight, down_weight, gate_mask, up_mask, down_mask):
    wide_tok = tokens.astype(jnp.float32)
    scale_inv = lax.rsqrt(jnp.mean(wide_tok * wide_tok, axis=-1, keepdims=True) + 1e-05)
    normed = (wide_tok * scale_inv * norm_gain).astype(jnp.bfloat16)
    gate_own, up_own, down_own = (gate_weight, up_weight, down_weight)
    gate_flags, up_flags, down_flags = (gate_mask, up_mask, down_mask)
    gate_kept = mask_blocks(gate_own, gate_flags)
    up_kept = mask_blocks(up_own, up_flags)
    down_kept = mask_blocks(down_own, down_flags)
    piece = lax.all_gather(normed, "blk", axis=0, tiled=True)
    gate = jnp.dot(piece, gate_kept, preferred_element_type=jnp.float32)
    up_val = jnp.dot(piece, up_kept, preferred_element_type=jnp.float32)
    hidden = (jax.nn.silu(gate) * up_val).astype(jnp.bfloat16)
    summed = lax.psum_scatter(
        jnp.dot(hidden, down_kept, preferred_element_type=jnp.float32),
        "blk",
        scatter_dimension=0,
        tiled=True,
    )
    return summed.astype(jnp.bfloat16)


def solution(mesh):
    return jax.shard_map(
        local,
        mesh=mesh,
        in_specs=(
            P(("blk", "rows"), None),
            P(),
            P(None, "blk"),
            P(None, "blk"),
            P("blk", None),
            P(None, "blk"),
            P(None, "blk"),
            P("blk", None),
        ),
        out_specs=P(("blk", "rows"), None),
        check_vma=False,
    )
```

profile of v0, /device:TPU:2, one launch (start us, length us, event | category | flops | bytes accessed | tf_op | source)
XLA Modules:
  0.0 906.0 jit_solution(3152752560273212439)
XLA Ops:
  6.5 0.0 all-gather.3.cloned.1.call-start
  6.5 0.9 fusion.8
  7.5 1.5 fusion.11
  9.0 0.0 all-gather.3.cloned.1.call-update
  9.0 0.7 convert_element_type.23
  9.7 0.1 copy.11
  9.8 0.7 convert_element_type.24
  10.5 0.1 copy.12
  10.6 0.7 convert_element_type.26
  11.3 1.3 dynamic-slice
  13.2 119.6 %all-gather.3.cloned.1.call-done = bf16[128,2,8192]{2,1,0:T(2,128)(2,1)} async-done(((bf16[1,2,8192]{2,1,0:T(2,128)(2,1)}), bf16[128,2,8192]{2,1,0:T(2,128)(2,1)}) %all-gather.3.cloned.1.call-update) | async-done | bytes 4194320 | tf_op jit(solution)/shard_map/all_gather | solution.py:24
  132.8 7.2 reshape.22
  140.0 0.0 copy-start
  140.0 2.2 mul.64
  142.2 0.0 copy-done
  142.2 3.5 fusion.4
  145.7 2.2 mul.68
  147.9 3.4 fusion.7
  151.3 0.0 copy-start.1
  151.4 1.1 mul.72
  152.5 1.1 copy-done.1
  153.5 6.5 fusion
  160.0 737.6 %all-reduce.2 = bf16[256,8192]{1,0:T(8,128)(2,1)} all-reduce(f32[256,8192]{1,0:T(8,128)} %fusion), channel_id=2, replica_groups=mesh['blk'=128,'rows'=2] {'blk'}, use_global_device_ids=true, to_apply=%region_1.2.clone | all-reduce | flops 2097152 | bytes 12582912
  897.6 1.6 dynamic-slice_convert_fusion
  (1 shorter events, 0.0 us)
Async XLA Ops:
  6.5 126.2 %all-gather.3.cloned.1.call-start = ((), (), s32[]{:S(2)}) async-start(), calls=%async_computation | async-start | bytes 4227072 | tf_op jit(solution)/shard_map/all_gather | solution.py:24
  140.0 2.2 copy-start
  151.3 2.2 copy-start.1
Sparse Core Ops, SparseCore 0:
  10.9 121.7 all-gather.2
where the time goes:
time: 907 us; the launch traced here: 906 us
  blocking collectives  738 us (81%)
  waiting for transfers between devices  120 us (13%)
  local copies, waits for them, and re-layouts  16.9 us (2%)
  between operations  14.1 us (2%)
  matrix products  13.4 us (1%)
    unnamed x1, blocking collectives  738 us
    all_gather x1, waiting for transfers between devices, local(): piece = lax.all_gather(normed, 'blk', axis=0, tiled=True)  120 us
  transfers between devices with their start and end apart: 1, of which 1 were waited for; matrix products, arithmetic and copies ran while one was open for 0% of the time, Pallas kernels for 0%

commit v1 on v0

--- a/solution.py
+++ b/solution.py
@@ -21,7 +21,9 @@
     gate_kept = mask_blocks(gate_own, gate_flags)
     up_kept = mask_blocks(up_own, up_flags)
     down_kept = mask_blocks(down_own, down_flags)
-    piece = lax.all_gather(normed, "blk", axis=0, tiled=True)
+    piece = jnp.concatenate(
+        lax.all_to_all(jnp.stack([normed] * lax.axis_size("blk")), "blk", 0, 0), axis=0
+    )
     gate = jnp.dot(piece, gate_kept, preferred_element_type=jnp.float32)
     up_val = jnp.dot(piece, up_kept, preferred_element_type=jnp.float32)
     hidden = (jax.nn.silu(gate) * up_val).astype(jnp.bfloat16)

time: 907 us -> 884 us (0.975)
  waiting for transfers between devices: 120 us -> 95.7 us
  starting transfers between devices: 0.01 us -> 15.7 us
  between operations: 14.1 us -> 0.78 us
    all_gather x1 -> x0, waiting for transfers between devices: 120 us -> none  [local(): piece = lax.all_gather(normed, 'blk', axis=0, tiled=True)]
    all_to_all x0 -> x1, waiting for transfers between devices: none -> 95.7 us  [local(): lax.all_to_all(jnp.stack([normed] * lax.axis_size('blk')), 'blk', 0, 0)]
    all_to_all x0 -> x1, starting transfers between devices: none -> 15.7 us  [local(): lax.all_to_all(jnp.stack([normed] * lax.axis_size('blk')), 'blk', 0, 0)]
where the time goes in v1:
time: 884 us
  blocking collectives  734 us (83%)
  waiting for transfers between devices  95.7 us (11%)
  local copies, waits for them, and re-layouts  22.4 us (3%)
  starting transfers between devices  15.7 us (2%)
  matrix products  13.4 us (2%)
    unnamed x1, blocking collectives  734 us
    all_to_all x1, waiting for transfers between devices, local(): lax.all_to_all(jnp.stack([normed] * lax.axis_size('blk')), 'blk', 0, 0)  95.7 us
  transfers between devices with their start and end apart: 1, of which 1 were waited for; matrix products, arithmetic and copies ran while one was open for 0% of the time, Pallas kernels for 0%

profile of v1, /device:TPU:2, one launch (start us, length us, event | category | flops | bytes accessed | tf_op | source)
XLA Modules:
  0.0 883.7 jit_solution(16467784680221409643)
XLA Ops:
  0.0 0.9 fusion.8
  0.9 0.9 fusion.10
  1.8 6.2 stack.2
  8.0 0.0 copy-start.2
  8.0 0.0 copy-start.3
  8.0 0.0 copy-start.4
  8.0 0.0 copy-start.5
  8.0 15.7 %all-to-all-start = ((bf16[128,2,8192]{2,1,0:T(2,128)(2,1)}), bf16[128,2,8192]{2,1,0:T(2,128)(2,1)}, u32[]{:S(2)}, u32[]{:S(2)}) async-start(bf16[128,2,8192]{2,1,0:T(2,128)(2,1)} %stack.2), calls=%async_computation | async-start | bytes 8388608 | tf_op jit(solution)/shard_map/all_to_all | solution.py:25
  23.8 0.0 copy-done.2
  23.8 0.1 copy.11
  23.9 0.0 copy-done.3
  23.9 0.1 copy.12
  24.0 0.0 copy-done.4
  24.0 0.0 copy-done.5
  24.0 0.6 dynamic-slice
  25.3 95.7 %all-to-all-done = bf16[128,2,8192]{2,1,0:T(2,128)(2,1)} async-done(((bf16[128,2,8192]{2,1,0:T(2,128)(2,1)}), bf16[128,2,8192]{2,1,0:T(2,128)(2,1)}, u32[]{:S(2)}, u32[]{:S(2)}) %all-to-all-start) | async-done | bytes 4194336 | tf_op jit(solution)/shard_map/all_to_all | solution.py:25
  121.0 7.2 reshape.26
  128.2 0.0 copy-start
  128.2 2.2 mul.64
  130.5 0.0 copy-done
  130.5 3.4 fusion.4
  133.9 2.2 mul.68
  136.2 3.5 fusion.7
  139.6 0.0 copy-start.1
  139.6 1.1 mul.72
  140.8 1.1 copy-done.1
  141.8 6.5 fusion
  148.3 733.9 %all-reduce.2 = bf16[256,8192]{1,0:T(8,128)(2,1)} all-reduce(f32[256,8192]{1,0:T(8,128)} %fusion), channel_id=2, replica_groups=mesh['blk'=128,'rows'=2] {'blk'}, use_global_device_ids=true, to_apply=%region_1.2.clone | all-reduce | flops 2097152 | bytes 12582912
  882.2 1.6 dynamic-slice_convert_fusion
  (4 shorter events, 0.0 us)
Async XLA Ops:
  8.0 15.8 %copy-start.2 = (s32[64,2]{0,1:T(2,128)S(1)}, s32[64,2]{0,1:T(2,128)}, u32[]{:S(2)}) copy-start(s32[64,2]{0,1:T(2,128)} %param.13) | copy-start | bytes 1540
  8.0 15.9 %copy-start.3 = (s32[64,2]{0,1:T(2,128)S(1)}, s32[64,2]{0,1:T(2,128)}, u32[]{:S(2)}) copy-start(s32[64,2]{0,1:T(2,128)} %param.14) | copy-start | bytes 1540
  8.0 16.0 %copy-start.4 = (s32[2,64]{1,0:T(2,128)S(1)}, s32[2,64]{1,0:T(2,128)}, u32[]{:S(2)}) copy-start(s32[2,64]{1,0:T(2,128)} %param.15) | copy-start | bytes 1540
  8.0 16.0 %copy-start.5 = (u32[256]{0:T(256)S(1)}, u32[256]{0:T(256)}, u32[]{:S(2)}) copy-start(u32[256]{0:T(256)} %constant.16) | copy-start | bytes 3076
  8.0 113.0 %all-to-all-start = ((bf16[128,2,8192]{2,1,0:T(2,128)(2,1)}), bf16[128,2,8192]{2,1,0:T(2,128)(2,1)}, u32[]{:S(2)}, u32[]{:S(2)}) async-start(bf16[128,2,8192]{2,1,0:T(2,128)(2,1)} %stack.2), calls=%async_computation | async-start | bytes 8388608 | tf_op jit(solution)/shard_map/all_to_all | solution.py:25
  128.2 2.2 copy-start
  139.6 2.2 copy-start.1
